TPU v7x, 256 devices: a whole 4x4x8 slice. The times are simulated.
256 devices in a mesh: gx: 32 (over x, y, core), gy: 8 (over z).
Axes of the slice: x: 4, y: 4, z: 8, core: 2. Of those that a mesh axis runs over, the one named last changes fastest.
Arguments:
- leaf_load: bfloat16 [65536, 384], P(('gx', 'gy')), may hold values from -6 to 6
- front_zero: bfloat16 [65536, 8192], P(('gx', 'gy')), may hold values from -0.046875 to 0.046875
- front_one: bfloat16 [32768, 8192], P(('gx', 'gy')), may hold values from -0.046875 to 0.046875
- front_two: bfloat16 [16384, 8192], P(('gx', 'gy')), may hold values from -0.046875 to 0.046875
- front_root: bfloat16 [8192, 8192], P(('gx', 'gy')), may hold values from -0.046875 to 0.046875
- load_one: float32 [32768, 384], P(('gx', 'gy')), may hold values from -6 to 6
- load_two: float32 [16384, 384], P(('gx', 'gy')), may hold values from -6 to 6
- load_root: float32 [8192, 384], P(('gx', 'gy')), may hold values from -6 to 6
- map_one: int32 [8192, 2], replicated, may hold values from 0 to 255
- map_two: int32 [8192, 2], replicated, may hold values from 0 to 127
- map_root: int32 [8192, 2], replicated, may hold values from 0 to 63
- adjoint: float32 [64, 128, 384], P('gx', 'gy'), may hold values from -6 to 6
Outputs:
- root_solution: float32 [8192, 384], P(('gx', 'gy'))
- gradient: float32 [64, 128, 384], P('gx', 'gy')
All inputs are finite; a program needn't handle non-finite values.
Results may differ from a plain program's by a relative error of at most 0.0055.
Values may be sent and summed in bfloat16 or wider, within the bound.
No kernel may reach another device: no remote copies, remote signals or barrier semaphores. Data moves between devices by JAX's collectives and lax.ppermute only.
A program may use at most 64 MiB of HBM per device.

v0:
```python
import jax
import jax.numpy as jnp
from jax import lax
from jax.sharding import PartitionSpec as P


def swapped(x, axis, distance):
    return lax.ppermute(x, axis, [(i, i ^ 1 << distance) for i in range(lax.axis_size(axis))])


def padded_2(cells, sides, width):
    for axis, dim in sides:
        count = lax.axis_size(axis)
        ends = count - 1
        head = lax.slice_in_dim(cells, 0, width, axis=dim)
        tail = lax.slice_in_dim(cells, cells.shape[dim] - width, cells.shape[dim], axis=dim)
        cells = jnp.concatenate(
            [
                lax.ppermute(tail, axis, [(i, (i + 1) % count) for i in range(ends)]),
                cells,
                lax.ppermute(head, axis, [((i + 1) % count, i) for i in range(ends)]),
            ],
            axis=dim,
        )
    return cells


def group_rows(values, bits):
    values = lax.all_gather(values, "gy", axis=0, tiled=True)
    column = lax.axis_index("gx")
    for bit in range(bits):
        other = swapped(values, "gx", bit)
        upper = column >> bit & 1 == 1
        values = jnp.where(
            upper, jnp.concatenate([other, values], 0), jnp.concatenate([values, other], 0)
        )
    return values


def local(
    leaf_load,
    front_zero,
    front_one,
    front_two,
    front_root,
    load_one,
    load_two,
    load_root,
    map_one,
    map_two,
    map_root,
    adjoint,
):
    leaf_bits = lax.axis_size("gx").bit_length() - 4
    fronts = (front_zero, front_one, front_two)
    loads = (load_one, load_two, load_root)
    mappings = (map_one, map_two, map_root)
    column = lax.axis_index("gx")
    row_index = lax.axis_index("gy")
    state = leaf_load
    for level in range(3):
        bits = leaf_bits + level
        whole = group_rows(state, bits)
        product = jnp.dot(fronts[level], whole, preferred_element_type=jnp.float32)
        other = swapped(product, "gx", bits)
        upper = column >> bits & 1 == 1
        first = jnp.where(upper, other, product)
        second = jnp.where(upper, product, other)
        half = product.shape[0] // 2
        position = column % 2 ** (bits + 1) * lax.axis_size("gy") + row_index
        local_map = lax.dynamic_slice_in_dim(mappings[level], position * half, half, 0)
        total = (
            loads[level]
            + jnp.take(first, local_map[:, 0], axis=0)
            + jnp.take(second, local_map[:, 1], axis=0)
        )
        state = total.astype(jnp.bfloat16)
    whole = group_rows(state, leaf_bits + 3)
    root_solution = jnp.dot(front_root, whole, preferred_element_type=jnp.float32)
    cells_x = adjoint.shape[0]
    cells_y = adjoint.shape[1]
    width = adjoint.shape[2]
    plane = root_solution.reshape(cells_x, cells_y, width)
    stacked = jnp.stack([plane, adjoint])
    padded = padded_2(stacked, (("gx", 1), ("gy", 2)), 1)
    padded_u = padded[0]
    padded_a = padded[1]
    gradient = jnp.zeros((cells_x, cells_y, width), jnp.float32)
    for lo_x, lo_y in ((2, 1), (0, 1), (1, 2), (1, 0)):
        near_u = padded_u[lo_x : lo_x + cells_x, lo_y : lo_y + cells_y]
        near_a = padded_a[lo_x : lo_x + cells_x, lo_y : lo_y + cells_y]
        gradient = gradient + (plane - near_u) * (adjoint - near_a)
    return (root_solution, gradient)


def solution(mesh):
    in_specs = (
        P(("gx", "gy"), None),
        P(("gx", "gy"), None),
        P(("gx", "gy"), None),
        P(("gx", "gy"), None),
        P(("gx", "gy"), None),
        P(("gx", "gy"), None),
        P(("gx", "gy"), None),
        P(("gx", "gy"), None),
        P(),
        P(),
        P(),
        P("gx", "gy", None),
    )
    out_specs = (P(("gx", "gy"), None), P("gx", "gy", None))
    return jax.shard_map(local, mesh=mesh, in_specs=in_specs, out_specs=out_specs, check_vma=False)
```

profile of v0, /device:TPU:34, one launch (start us, length us, event | category | flops | bytes accessed | tf_op | source)
XLA Modules:
  0.0 686.3 jit_solution(2727871176709467057)
XLA Ops:
  7.9 44.2 %all-gather.2.cloned.1.call-done = bf16[2048,384]{1,0:T(8,128)(2,1)} async-done(((bf16[256,384]{1,0:T(8,128)(2,1)}), bf16[2048,384]{1,0:T(8,128)(2,1)}) %all-gather.2.cloned.1.call-update) | async-done | bytes 1572880 | tf_op jit(solution)/shard_map/all_gather | solution.py:29
  55.8 5.5 maximum_select_fusion.8
  62.8 69.0 %collective-permute-done.1 = bf16[4096,384]{1,0:T(8,128)(2,1)} collective-permute-done((bf16[4096,384]{1,0:T(8,128)(2,1)}, bf16[4096,384]{1,0:T(8,128)(2,1)}, u32[]{:S(2)}, u32[]{:S(2)}) %collective-permute-start.1) | collective-permute-done | bytes 3145760 | tf_op jit(solution)/shard_map/ppermute | solution.py:8
  131.8 9.1 %fusion.28 = f32[256,384]{0,1:T(8,128)S(1)} fusion(bf16[256,8192]{1,0:T(8,128)(2,1)} %param.19, bf16[4096,384]{1,0:T(8,128)(2,1)} %maximum_select_fusion.8, bf16[4096,384]{1,0:T(8,128)(2,1)} %collective-permute-done.1, pred[]{:T(512)S(6)} %eq.17), kind=kOutput, calls=%fused_computation.45 | convolution fusion | flops 1638924288 | bytes 10878977 | tf_op jit(solution)/shard_map/dot_general | solution.py:64
  144.7 8.1 %collective-permute-done.2 = f32[256,384]{0,1:T(8,128)S(1)} collective-permute-done((f32[256,384]{0,1:T(8,128)S(1)}, f32[256,384]{0,1:T(8,128)S(1)}, u32[]{:S(2)}, u32[]{:S(2)}) %collective-permute-start.2) | collective-permute-done | bytes 393248 | tf_op jit(solution)/shard_map/ppermute | solution.py:8
  154.8 25.7 %all_gather.13 = bf16[1024,384]{1,0:T(8,128)(2,1)S(1)} all-gather(bf16[128,384]{1,0:T(8,128)(2,1)S(1)} %fusion.31), channel_id=1, replica_groups=mesh['gx'=32,'gy'=8] {'gy'}, dimensions={0}, use_global_device_ids=true | all-gather | bytes 884736 | tf_op jit(solution)/shard_map/all_gather | solution.py:29
  184.8 35.0 %collective-permute-done.4 = bf16[2048,384]{1,0:T(8,128)(2,1)S(1)} collective-permute-done((bf16[2048,384]{1,0:T(8,128)(2,1)S(1)}, bf16[2048,384]{1,0:T(8,128)(2,1)S(1)}, u32[]{:S(2)}, u32[]{:S(2)}) %collective-permute-start.4) | collective-permute-done | bytes 1572896 | tf_op jit(solution)/shard_map/ppermute | solution.py:8
  219.8 8.3 %maximum_select_fusion.9 = bf16[4096,384]{1,0:T(8,128)(2,1)} fusion(bf16[2048,384]{1,0:T(8,128)(2,1)S(1)} %maximum_select_fusion.12, bf16[2048,384]{1,0:T(8,128)(2,1)S(1)} %collective-permute-done.4, pred[]{:T(512)S(6)} %eq.17), kind=kLoop, calls=%fused_computation.39 | loop fusion | flops 14155776 | bytes 6291457 | tf_op jit(solution)/shard_map/jit(_where)/select_n | solution.py:34
  231.8 67.4 %collective-permute-done.5 = bf16[4096,384]{1,0:T(8,128)(2,1)} collective-permute-done((bf16[4096,384]{1,0:T(8,128)(2,1)}, bf16[4096,384]{1,0:T(8,128)(2,1)}, u32[]{:S(2)}, u32[]{:S(2)}) %collective-permute-start.5) | collective-permute-done | bytes 3145760 | tf_op jit(solution)/shard_map/ppermute | solution.py:8
  299.2 6.3 fusion.29
  306.4 5.1 collective-permute-done.6
  313.2 25.2 %all_gather.14 = bf16[512,384]{1,0:T(8,128)(2,1)S(1)} all-gather(bf16[64,384]{1,0:T(8,128)(2,1)S(1)} %fusion.32), channel_id=1, replica_groups=mesh['gx'=32,'gy'=8] {'gy'}, dimensions={0}, use_global_device_ids=true | all-gather | bytes 442368 | tf_op jit(solution)/shard_map/all_gather | solution.py:29
  342.0 18.1 %collective-permute-done.8 = bf16[1024,384]{1,0:T(8,128)(2,1)S(1)} collective-permute-done((bf16[1024,384]{1,0:T(8,128)(2,1)S(1)}, bf16[1024,384]{1,0:T(8,128)(2,1)S(1)}, u32[]{:S(2)}, u32[]{:S(2)}) %collective-permute-start.8) | collective-permute-done | bytes 786464 | tf_op jit(solution)/shard_map/ppermute | solution.py:8
  363.6 34.1 %collective-permute-done.9 = bf16[2048,384]{1,0:T(8,128)(2,1)S(1)} collective-permute-done((bf16[2048,384]{1,0:T(8,128)(2,1)S(1)}, bf16[2048,384]{1,0:T(8,128)(2,1)S(1)}, u32[]{:S(2)}, u32[]{:S(2)}) %collective-permute-start.9) | collective-permute-done | bytes 1572896 | tf_op jit(solution)/shard_map/ppermute | solution.py:8
  397.7 8.3 %maximum_select_fusion.10 = bf16[4096,384]{1,0:T(8,128)(2,1)} fusion(bf16[2048,384]{1,0:T(8,128)(2,1)S(1)} %maximum_select_fusion.13, bf16[2048,384]{1,0:T(8,128)(2,1)S(1)} %collective-permute-done.9, pred[]{:T(512)S(6)} %eq.16), kind=kLoop, calls=%fused_computation.40 | loop fusion | flops 14155776 | bytes 6291457 | tf_op jit(solution)/shard_map/jit(_where)/select_n | solution.py:34
  407.3 67.4 %collective-permute-done.10 = bf16[4096,384]{1,0:T(8,128)(2,1)} collective-permute-done((bf16[4096,384]{1,0:T(8,128)(2,1)}, bf16[4096,384]{1,0:T(8,128)(2,1)}, u32[]{:S(2)}, u32[]{:S(2)}) %collective-permute-start.10) | collective-permute-done | bytes 3145760 | tf_op jit(solution)/shard_map/ppermute | solution.py:8
  474.7 6.2 fusion.30
  488.5 24.8 %all_gather.15 = bf16[256,384]{1,0:T(8,128)(2,1)S(1)} all-gather(bf16[32,384]{1,0:T(8,128)(2,1)S(1)} %fusion.41), channel_id=1, replica_groups=mesh['gx'=32,'gy'=8] {'gy'}, dimensions={0}, use_global_device_ids=true | all-gather | bytes 221184 | tf_op jit(solution)/shard_map/all_gather | solution.py:29
  516.4 9.7 %collective-permute-done.13 = bf16[512,384]{1,0:T(8,128)(2,1)S(1)} collective-permute-done((bf16[512,384]{1,0:T(8,128)(2,1)S(1)}, bf16[512,384]{1,0:T(8,128)(2,1)S(1)}, u32[]{:S(2)}, u32[]{:S(2)}) %collective-permute-start.13) | collective-permute-done | bytes 393248 | tf_op jit(solution)/shard_map/ppermute | solution.py:8
  529.5 17.2 %collective-permute-done.14 = bf16[1024,384]{1,0:T(8,128)(2,1)S(1)} collective-permute-done((bf16[1024,384]{1,0:T(8,128)(2,1)S(1)}, bf16[1024,384]{1,0:T(8,128)(2,1)S(1)}, u32[]{:S(2)}, u32[]{:S(2)}) %collective-permute-start.14) | collective-permute-done | bytes 786464 | tf_op jit(solution)/shard_map/ppermute | solution.py:8
  548.1 34.1 %collective-permute-done.15 = bf16[2048,384]{1,0:T(8,128)(2,1)S(1)} collective-permute-done((bf16[2048,384]{1,0:T(8,128)(2,1)S(1)}, bf16[2048,384]{1,0:T(8,128)(2,1)S(1)}, u32[]{:S(2)}, u32[]{:S(2)}) %collective-permute-start.15) | collective-permute-done | bytes 1572896 | tf_op jit(solution)/shard_map/ppermute | solution.py:8
  582.2 7.2 %maximum_select_fusion.11 = bf16[4096,384]{1,0:T(8,128)(2,1)S(1)} fusion(bf16[2048,384]{1,0:T(8,128)(2,1)S(1)} %maximum_select_fusion.14, bf16[2048,384]{1,0:T(8,128)(2,1)S(1)} %collective-permute-done.15, pred[]{:T(512)S(6)} %eq.15), kind=kLoop, calls=%fused_computation.41 | loop fusion | flops 14155776 | bytes 6291457 | tf_op jit(solution)/shard_map/jit(_where)/select_n | solution.py:34
  591.6 66.9 %collective-permute-done.16 = bf16[4096,384]{1,0:T(8,128)(2,1)S(1)} collective-permute-done((bf16[4096,384]{1,0:T(8,128)(2,1)S(1)}, bf16[4096,384]{1,0:T(8,128)(2,1)S(1)}, u32[]{:S(2)}, u32[]{:S(2)}) %collective-permute-start.16) | collective-permute-done | bytes 3145760 | tf_op jit(solution)/shard_map/ppermute | solution.py:8
  664.7 5.1 collective-permute-done.17
  (84 shorter events, 64.1 us)
Async XLA Ops:
  7.2 292.0 %copy-start = (bf16[128,8192]{1,0:T(8,128)(2,1)S(1)}, bf16[128,8192]{1,0:T(8,128)(2,1)}, u32[]{:S(2)}) copy-start(bf16[128,8192]{1,0:T(8,128)(2,1)} %param.20) | copy-start | bytes 6291460
  7.2 44.9 %all-gather.2.cloned.1.call-start = ((), (), s32[]{:S(2)}) async-start(), calls=%async_computation | async-start | bytes 1769472 | tf_op jit(solution)/shard_map/all_gather | solution.py:29
  52.1 3.8 collective-permute-start
  61.3 70.5 %collective-permute-start.1 = (bf16[4096,384]{1,0:T(8,128)(2,1)}, bf16[4096,384]{1,0:T(8,128)(2,1)}, u32[]{:S(2)}, u32[]{:S(2)}) collective-permute-start(bf16[4096,384]{1,0:T(8,128)(2,1)} %maximum_select_fusion.8), channel_id=1, source_target_pairs={{0,16},{8,24},{16,0},{24,8},{32,48},{40,56},{48,32},{56,40},{64,80... | collective-permute-start | bytes 9437192 | tf_op jit(solution)/shard_map/ppermute | solution.py:8
  140.8 11.9 %collective-permute-start.2 = (f32[256,384]{0,1:T(8,128)S(1)}, f32[256,384]{0,1:T(8,128)S(1)}, u32[]{:S(2)}, u32[]{:S(2)}) collective-permute-start(f32[256,384]{0,1:T(8,128)S(1)} %fusion.28), channel_id=1, source_target_pairs={{0,32},{8,40},{16,48},{24,56},{32,0},{40,8},{48,16},{56,24},{64,96... | collective-permute-start | bytes 1179656 | tf_op jit(solution)/shard_map/ppermute | solution.py:8
  180.5 2.3 collective-permute-start.3
  183.2 36.5 %collective-permute-start.4 = (bf16[2048,384]{1,0:T(8,128)(2,1)S(1)}, bf16[2048,384]{1,0:T(8,128)(2,1)S(1)}, u32[]{:S(2)}, u32[]{:S(2)}) collective-permute-start(bf16[2048,384]{1,0:T(8,128)(2,1)S(1)} %maximum_select_fusion.12), channel_id=1, source_target_pairs={{0,16},{8,24},{16,0},{24,8},{32,48},{40,56},{48,32},{56,40},{64,80... | collective-permute-start | bytes 4718600 | tf_op jit(solution)/shard_map/ppermute | solution.py:8
  228.0 71.1 %collective-permute-start.5 = (bf16[4096,384]{1,0:T(8,128)(2,1)}, bf16[4096,384]{1,0:T(8,128)(2,1)}, u32[]{:S(2)}, u32[]{:S(2)}) collective-permute-start(bf16[4096,384]{1,0:T(8,128)(2,1)} %maximum_select_fusion.9), channel_id=1, source_target_pairs={{0,32},{8,40},{16,48},{24,56},{32,0},{40,8},{48,16},{56,24},{64,96... | collective-permute-start | bytes 9437192 | tf_op jit(solution)/shard_map/ppermute | solution.py:8
  305.5 5.9 collective-permute-start.6
  338.4 1.7 collective-permute-start.7
  340.4 19.7 %collective-permute-start.8 = (bf16[1024,384]{1,0:T(8,128)(2,1)S(1)}, bf16[1024,384]{1,0:T(8,128)(2,1)S(1)}, u32[]{:S(2)}, u32[]{:S(2)}) collective-permute-start(bf16[1024,384]{1,0:T(8,128)(2,1)S(1)} %maximum_select_fusion.21), channel_id=1, source_target_pairs={{0,16},{8,24},{16,0},{24,8},{32,48},{40,56},{48,32},{56,40},{64,80... | collective-permute-start | bytes 2359304 | tf_op jit(solution)/shard_map/ppermute | solution.py:8
  360.5 114.2 %copy-start.6 = (bf16[64,8192]{1,0:T(8,128)(2,1)S(1)}, bf16[64,8192]{1,0:T(8,128)(2,1)}, u32[]{:S(2)}) copy-start(bf16[64,8192]{1,0:T(8,128)(2,1)} %param.21) | copy-start | bytes 3145732
  360.5 37.2 %collective-permute-start.9 = (bf16[2048,384]{1,0:T(8,128)(2,1)S(1)}, bf16[2048,384]{1,0:T(8,128)(2,1)S(1)}, u32[]{:S(2)}, u32[]{:S(2)}) collective-permute-start(bf16[2048,384]{1,0:T(8,128)(2,1)S(1)} %maximum_select_fusion.13), channel_id=1, source_target_pairs={{0,32},{8,40},{16,48},{24,56},{32,0},{40,8},{48,16},{56,24},{64,96... | collective-permute-start | bytes 4718600 | tf_op jit(solution)/shard_map/ppermute | solution.py:8
  406.0 68.7 %collective-permute-start.10 = (bf16[4096,384]{1,0:T(8,128)(2,1)}, bf16[4096,384]{1,0:T(8,128)(2,1)}, u32[]{:S(2)}, u32[]{:S(2)}) collective-permute-start(bf16[4096,384]{1,0:T(8,128)(2,1)} %maximum_select_fusion.10), channel_id=1, source_target_pairs={{0,64},{8,72},{16,80},{24,88},{32,96},{40,104},{48,112},{56,120},{... | collective-permute-start | bytes 9437192 | tf_op jit(solution)/shard_map/ppermute | solution.py:8
  480.9 6.2 collective-permute-start.11
  513.3 1.4 collective-permute-start.12
  514.9 11.2 %collective-permute-start.13 = (bf16[512,384]{1,0:T(8,128)(2,1)S(1)}, bf16[512,384]{1,0:T(8,128)(2,1)S(1)}, u32[]{:S(2)}, u32[]{:S(2)}) collective-permute-start(bf16[512,384]{1,0:T(8,128)(2,1)S(1)} %maximum_select_fusion.23), channel_id=1, source_target_pairs={{0,16},{8,24},{16,0},{24,8},{32,48},{40,56},{48,32},{56,40},{64,80... | collective-permute-start | bytes 1179656 | tf_op jit(solution)/shard_map/ppermute | solution.py:8
  526.4 20.3 %collective-permute-start.14 = (bf16[1024,384]{1,0:T(8,128)(2,1)S(1)}, bf16[1024,384]{1,0:T(8,128)(2,1)S(1)}, u32[]{:S(2)}, u32[]{:S(2)}) collective-permute-start(bf16[1024,384]{1,0:T(8,128)(2,1)S(1)} %maximum_select_fusion.22), channel_id=1, source_target_pairs={{0,32},{8,40},{16,48},{24,56},{32,0},{40,8},{48,16},{56,24},{64,96... | collective-permute-start | bytes 2359304 | tf_op jit(solution)/shard_map/ppermute | solution.py:8
  547.2 35.0 %collective-permute-start.15 = (bf16[2048,384]{1,0:T(8,128)(2,1)S(1)}, bf16[2048,384]{1,0:T(8,128)(2,1)S(1)}, u32[]{:S(2)}, u32[]{:S(2)}) collective-permute-start(bf16[2048,384]{1,0:T(8,128)(2,1)S(1)} %maximum_select_fusion.14), channel_id=1, source_target_pairs={{0,64},{8,72},{16,80},{24,88},{32,96},{40,104},{48,112},{56,120},{... | collective-permute-start | bytes 4718600 | tf_op jit(solution)/shard_map/ppermute | solution.py:8
  589.4 69.1 %collective-permute-start.16 = (bf16[4096,384]{1,0:T(8,128)(2,1)S(1)}, bf16[4096,384]{1,0:T(8,128)(2,1)S(1)}, u32[]{:S(2)}, u32[]{:S(2)}) collective-permute-start(bf16[4096,384]{1,0:T(8,128)(2,1)S(1)} %maximum_select_fusion.11), channel_id=1, source_target_pairs={{0,128},{8,136},{16,144},{24,152},{32,160},{40,168},{48,176},{56,1... | collective-permute-start | bytes 9437192 | tf_op jit(solution)/shard_map/ppermute | solution.py:8
  660.3 4.3 collective-permute-start.18
  662.3 7.5 %collective-permute-start.17 = (f32[2,1,16,384]{3,2,1,0:T(8,128)S(1)}, f32[2,1,16,384]{3,2,1,0:T(8,128)S(1)}, u32[]{:S(2)}, u32[]{:S(2)}) collective-permute-start(f32[2,1,16,384]{3,2,1,0:T(8,128)S(1)} %get-tuple-element.27), channel_id=1, source_target_pairs={{0,8},{8,16},{16,24},{24,32},{32,40},{40,48},{48,56},{56,64},{64,7... | collective-permute-start | bytes 147464 | tf_op jit(solution)/shard_map/ppermute | solution.py:19
  669.8 5.9 collective-permute-start.20
  673.1 5.6 collective-permute-start.19
  (6 other events, 300.0 us)
Sparse Core Ops, SparseCore 0:
  9.8 42.2 all-gather.1
where the time goes:
time: 687 us; the launch traced here: 686 us
  waiting for transfers between devices  498 us (72%)
  blocking collectives  75.7 us (11%)
  starting transfers between devices  35.3 us (5%)
  other arithmetic  32.4 us (5%)
  matrix products  23.4 us (3%)
  between operations  14.4 us (2%)
  local copies, waits for them, and re-layouts  6.91 us (1%)
    ppermute x17, waiting for transfers between devices, swapped(): lax.ppermute(x, axis, [(i, i ^ 1 << distance) for i in range(lax.axis_siz...  445 us
    all_gather x3, blocking collectives, group_rows(): values = lax.all_gather(values, 'gy', axis=0, tiled=True)  75.7 us
    all_gather x1, waiting for transfers between devices, group_rows(): values = lax.all_gather(values, 'gy', axis=0, tiled=True)  44.2 us
    select_n x10, other arithmetic, group_rows(): jnp.where(upper, jnp.concatenate([other, values], 0), jnp.concatenate([va...  31.2 us
    ppermute x17, starting transfers between devices, swapped(): lax.ppermute(x, axis, [(i, i ^ 1 << distance) for i in range(lax.axis_siz...  25.1 us
    dot_general x3, matrix products, local(): product = jnp.dot(fronts[level], whole, preferred_element_type=jnp.float32)  21.6 us
  transfers between devices with their start and end apart: 22, of which 20 were waited for; matrix products, arithmetic and copies ran while one was open for 0% of the time, Pallas kernels for 0%

commit v1 on v0

v1 whole, which is shorter than its diff:
```python
import numpy as np
import jax
import jax.numpy as jnp
from jax import lax
from jax.sharding import Mesh, PartitionSpec as P

GX = ("xa", "ya", "c")
ALL = ("xa", "ya", "c", "gy")


def moved(x, axis, pairs):
    return lax.ppermute(x, axis, pairs)


def ring_blocks(x, axis, n, size):
    if n == 2 and size != 2:
        return jnp.stack([x, moved(x, axis, [(i, i ^ 1) for i in range(size)])])
    up = [(i, (i + 1) % n) for i in range(n)]
    down = [(i, (i - 1) % n) for i in range(n)]
    pieces = [None] * n
    pieces[0] = x
    fwd = x
    bwd = x
    for s in range(1, (n - 1) // 2 + 1):
        fwd = moved(fwd, axis, up)
        bwd = moved(bwd, axis, down)
        pieces[n - s] = fwd
        pieces[s] = bwd
    if n % 2 == 0:
        h = x.shape[0] // 2
        a = moved(fwd[:h], axis, up)
        b = moved(bwd[h:], axis, down)
        pieces[n // 2] = jnp.concatenate([a, b], 0)
    return jnp.stack(pieces)


def gather_front(block, dims, order):
    held = []
    x = block
    for name in order:
        axis, n, size, me = dims[name]
        x = ring_blocks(x, axis, n, size)
        held.insert(0, name)
    canon = [name for name in ("X", "Y", "Z") if name in dims]
    x = jnp.transpose(x, [held.index(name) for name in canon] + [len(held), len(held) + 1])
    for i, name in enumerate(canon):
        x = jnp.roll(x, dims[name][3], axis=i)
    return x.reshape(-1, x.shape[-1])


def level_dims(level, sizes, idx):
    nxa, nya, ngy = sizes
    xa, ya, gy = idx
    dims = {"Z": ("gy", ngy, ngy, gy)}
    if level == 0:
        dims["Y"] = ("ya", 2, nya, ya % 2)
    else:
        dims["Y"] = ("ya", nya, nya, ya)
    if level == 2:
        dims["X"] = ("xa", 2, nxa, xa % 2)
    elif level == 3:
        dims["X"] = ("xa", nxa, nxa, xa)
    return dims


ORDERS = {
    0: (("Z", "Y"), ("Y", "Z")),
    1: (("Z", "Y"), ("Y", "Z")),
    2: (("Z", "Y", "X"), ("X", "Z", "Y"), ("Y", "X", "Z")),
    3: (("Z", "Y", "X"), ("X", "Z", "Y"), ("Y", "X", "Z")),
}


def split_columns(front, core, groups):
    rows = front.shape[0]
    four = front.reshape(rows, groups, 2, -1)
    mine = lax.dynamic_index_in_dim(four, core, axis=2, keepdims=False).reshape(rows, -1)
    theirs = lax.dynamic_index_in_dim(four, 1 - core, axis=2, keepdims=False).reshape(rows, -1)
    return mine, moved(theirs, "c", [(0, 1), (1, 0)])


def apply_front(front_parts, state, level, sizes, idx):
    own_a, other_a = front_parts
    dims = level_dims(level, sizes, idx)
    orders = ORDERS[level]
    width = state.shape[1]
    count = len(orders)
    edges = [width * i // count // 128 * 128 for i in range(count)] + [width]
    mine = []
    theirs = []
    for i, order in enumerate(orders):
        part = state[:, edges[i] : edges[i + 1]]
        whole = gather_front(part, dims, order)
        mine.append(jnp.dot(own_a, whole, preferred_element_type=jnp.float32))
        theirs.append(jnp.dot(other_a, whole, preferred_element_type=jnp.float32))
    mine = jnp.concatenate(mine, 1)
    theirs = jnp.concatenate(theirs, 1)
    return mine + moved(theirs, "c", [(0, 1), (1, 0)])


def padded_2(cells, sides, width):
    for axis, count, dim in sides:
        ends = count - 1
        head = lax.slice_in_dim(cells, 0, width, axis=dim)
        tail = lax.slice_in_dim(cells, cells.shape[dim] - width, cells.shape[dim], axis=dim)
        cells = jnp.concatenate(
            [
                lax.ppermute(tail, axis, [(i, (i + 1) % count) for i in range(ends)]),
                cells,
                lax.ppermute(head, axis, [((i + 1) % count, i) for i in range(ends)]),
            ],
            axis=dim,
        )
    return cells


def make_local(sizes):
    nxa, nya, ngy = sizes
    ngx = nxa * nya * 2
    leaf_bits = ngx.bit_length() - 4

    def local(
        leaf_load,
        front_zero,
        front_one,
        front_two,
        front_root,
        load_one,
        load_two,
        load_root,
        map_one,
        map_two,
        map_root,
        adjoint,
    ):
        fronts = (front_zero, front_one, front_two, front_root)
        loads = (load_one, load_two, load_root)
        mappings = (map_one, map_two, map_root)
        xa = lax.axis_index("xa")
        ya = lax.axis_index("ya")
        core = lax.axis_index("c")
        row_index = lax.axis_index("gy")
        column = (xa * nya + ya) * 2 + core
        idx = (xa, ya, row_index)
        groups = (1, 1, 2, nxa)
        parts = [
            split_columns(fronts[level], core, groups[level] * (nya if level else 2))
            for level in range(4)
        ]
        state = leaf_load
        for level in range(3):
            bits = leaf_bits + level
            product = apply_front(parts[level], state, level, sizes, idx)
            other = moved(product, GX, [(i, i ^ 1 << bits) for i in range(ngx)])
            upper = column >> bits & 1 == 1
            first = jnp.where(upper, other, product)
            second = jnp.where(upper, product, other)
            half = product.shape[0] // 2
            position = column % 2 ** (bits + 1) * ngy + row_index
            local_map = lax.dynamic_slice_in_dim(mappings[level], position * half, half, 0)
            total = (
                loads[level]
                + jnp.take(first, local_map[:, 0], axis=0)
                + jnp.take(second, local_map[:, 1], axis=0)
            )
            state = total.astype(jnp.bfloat16)
        root_solution = apply_front(parts[3], state, 3, sizes, idx)
        cells_x = adjoint.shape[0]
        cells_y = adjoint.shape[1]
        width = adjoint.shape[2]
        plane = root_solution.reshape(cells_x, cells_y, width)
        stacked = jnp.stack([plane, adjoint])
        padded = padded_2(stacked, ((GX, ngx, 1), ("gy", ngy, 2)), 1)
        padded_u = padded[0]
        padded_a = padded[1]
        gradient = jnp.zeros((cells_x, cells_y, width), jnp.float32)
        for lo_x, lo_y in ((2, 1), (0, 1), (1, 2), (1, 0)):
            near_u = padded_u[lo_x : lo_x + cells_x, lo_y : lo_y + cells_y]
            near_a = padded_a[lo_x : lo_x + cells_x, lo_y : lo_y + cells_y]
            gradient = gradient + (plane - near_u) * (adjoint - near_a)
        return (root_solution, gradient)

    return local


def solution(mesh):
    ngx = mesh.shape["gx"]
    ngy = mesh.shape["gy"]
    nya = 4
    nxa = ngx // (2 * nya)
    devices = np.asarray(mesh.devices).reshape(nxa, nya, 2, ngy)
    fine = Mesh(devices, ALL)
    rows = P(ALL, None)
    in_specs = (rows,) * 8 + (P(), P(), P(), P(GX, "gy", None))
    out_specs = (rows, P(GX, "gy", None))
    return jax.shard_map(
        make_local((nxa, nya, ngy)), mesh=fine, in_specs=in_specs, out_specs=out_specs, check_vma=False
    )
```

time: 687 us -> 417 us (0.61)
  waiting for transfers between devices: 498 us -> 131 us
  starting transfers between devices: 35.3 us -> 204 us
  blocking collectives: 75.7 us -> 0 us
  local copies, waits for them, and re-layouts: 6.91 us -> 42.3 us
  other arithmetic: 32.4 us -> 16.1 us
  between operations: 14.4 us -> 2.99 us
  matrix products: 23.4 us -> 14.5 us
    ppermute x17 -> x140, waiting for transfers between devices: 445 us -> 127 us  [moved(): return lax.ppermute(x, axis, pairs)]
    ppermute x17 -> x140, starting transfers between devices: 25.1 us -> 190 us  [moved(): return lax.ppermute(x, axis, pairs)]
    all_gather x3 -> x0, blocking collectives: 75.7 us -> none  [group_rows(): values = lax.all_gather(values, 'gy', axis=0, tiled=True)]
    all_gather x1 -> x0, waiting for transfers between devices: 44.2 us -> none  [group_rows(): values = lax.all_gather(values, 'gy', axis=0, tiled=True)]
    select_n x10 -> x0, other arithmetic: 31.2 us -> none  [group_rows(): jnp.where(upper, jnp.concatenate([other, values], 0), jnp.concatenate([va...]
    dynamic_slice x0 -> x10, local copies, waits for them, and re-layouts: none -> 17.2 us  [the longest x4 16.6 us: split_columns(): lax.dynamic_index_in_dim(four, core, axis=2, keepdims=False)]
    unnamed x16 -> x87, local copies, waits for them, and re-layouts: 0.06 us -> 13.5 us
    concatenate x0 -> x29, other arithmetic: none -> 12.9 us  [the longest x25 12.9 us: gather_front(): x = jnp.roll(x, dims[name][3], axis=i)]
  transfers between devices with their start and end apart: 22 -> 144, of which waited for: 20 -> 45; matrix products, arithmetic and copies ran while one was open for 0% -> 16% of each run, Pallas kernels for 0% -> 0%
where the time goes in v1:
time: 417 us; the launch traced here: 411 us
  starting transfers between devices  204 us (49%)
  waiting for transfers between devices  131 us (31%)
  local copies, waits for them, and re-layouts  42.3 us (10%)
  other arithmetic  16.1 us (4%)
  matrix products  14.5 us (3%)
    ppermute x140, starting transfers between devices, moved(): return lax.ppermute(x, axis, pairs)  190 us
    ppermute x140, waiting for transfers between devices, moved(): return lax.ppermute(x, axis, pairs)  127 us
    dynamic_slice x4, local copies, waits for them, and re-layouts, split_columns(): lax.dynamic_index_in_dim(four, core, axis=2, keepdims=False)  16.6 us
    unnamed x87, local copies, waits for them, and re-layouts  13.5 us
    concatenate x25, other arithmetic, gather_front(): x = jnp.roll(x, dims[name][3], axis=i)  12.9 us
    dot_general x10, matrix products, apply_front(): theirs.append(jnp.dot(other_a, whole, preferred_element_type=jnp.float32))  10.1 us
    ppermute x2, starting transfers between devices, padded_2(): lax.ppermute(head, axis, [((i + 1) % count, i) for i in range(ends)])  9.87 us
  transfers between devices with their start and end apart: 144, of which 45 were waited for; matrix products, arithmetic and copies ran while one was open for 16% of the time, Pallas kernels for 0%

profile of v1, /device:TPU:34, one launch (start us, length us, event | category | flops | bytes accessed | tf_op | source)
XLA Modules:
  0.0 411.0 jit_solution(9113111730983447920)
XLA Ops:
  7.3 6.4 %copy.41 = bf16[256,8192]{0,1:T(8,128)(2,1)} copy(bf16[256,8192]{1,0:T(8,128)(2,1)} %param.31) | data formatting | bytes 8388608 | tf_op args[1]
  13.7 4.7 %constant_dynamic-slice_fusion.6 = (bf16[256,2,1,2048]{0,3,2,1:T(8,128)(2,1)}, bf16[256,2,1,2048]{0,3,2,1:T(8,128)(2,1)}) fusion(bf16[256,2,2,2048]{0,3,2,1:T(8,128)(2,1)} %bitcast.378, s32[]{:T(128)S(6)} %select_n.209, s32[]{:T(128)S(6)} %select_n.218), kind=kLoop, calls=%fused_computation.272 | loop fusion | bytes 8388616 | tf_op jit(solution)/shard_map/jit(dynamic_index_in_dim)/dynamic_slice | solution.py:77
  27.0 6.2 %dynamic-slice_reduce_fusion.1 = (bf16[64,8,512]{2,1,0:T(8,128)(2,1)S(1)}, bf16[64,8,512]{2,1,0:T(8,128)(2,1)S(1)}) fusion(bf16[64,8,2,512]{3,2,1,0:T(2,128)(2,1)S(1)} %reshape.98, s32[]{:T(128)S(6)} %select_n.209, s32[]{:T(128)S(6)} %select_n.218), kind=kLoop, calls=%fused_computation.104 | loop fusion | bytes 2097160 | tf_op jit(solution)/shard_map/jit(dynamic_index_in_dim)/dynamic_slice | solution.py:77
  39.5 4.4 %collective-permute-start.1 = (bf16[256,128]{1,0:T(8,128)(2,1)}, bf16[256,128]{1,0:T(8,128)(2,1)S(1)}, u32[]{:S(2)}, u32[]{:S(2)}) collective-permute-start(bf16[256,128]{1,0:T(8,128)(2,1)} %collective-permute-done), channel_id=1, source_target_pairs={{0,7},{1,0},{2,1},{3,2},{4,3},{5,4},{6,5},{7,6},{8,15},{9,8},{10,9... | collective-permute-start | bytes 196616 | tf_op jit(solution)/shard_map/ppermute | solution.py:12
  51.4 4.2 %collective-permute-done.5 = bf16[256,128]{1,0:T(8,128)(2,1)S(1)} collective-permute-done((bf16[256,128]{1,0:T(8,128)(2,1)S(1)}, bf16[256,128]{1,0:T(8,128)(2,1)S(1)}, u32[]{:S(2)}, u32[]{:S(2)}) %collective-permute-start.5) | collective-permute-done | bytes 65568 | tf_op jit(solution)/shard_map/ppermute | solution.py:12
  64.0 4.1 %collective-permute-done.13 = bf16[2,256,256]{2,1,0:T(8,128)(2,1)S(1)} collective-permute-done((bf16[2,256,256]{2,1,0:T(8,128)(2,1)S(1)}, bf16[2,256,256]{2,1,0:T(8,128)(2,1)S(1)}, u32[]{:S(2)}, u32[]{:S(2)}) %collective-permute-start.13) | collective-permute-done | bytes 262176 | tf_op jit(solution)/shard_map/ppermute | solution.py:12
  71.8 5.7 %collective-permute-done.14 = bf16[2,256,256]{2,1,0:T(8,128)(2,1)S(1)} collective-permute-done((bf16[2,256,256]{2,1,0:T(8,128)(2,1)S(1)}, bf16[2,256,256]{2,1,0:T(8,128)(2,1)S(1)}, u32[]{:S(2)}, u32[]{:S(2)}) %collective-permute-start.14) | collective-permute-done | bytes 262176 | tf_op jit(solution)/shard_map/ppermute | solution.py:12
  78.7 8.1 %collective-permute-done.15 = bf16[2,256,256]{2,1,0:T(8,128)(2,1)S(1)} collective-permute-done((bf16[2,256,256]{2,1,0:T(8,128)(2,1)S(1)}, bf16[2,256,256]{2,1,0:T(8,128)(2,1)S(1)}, u32[]{:S(2)}, u32[]{:S(2)}) %collective-permute-start.15) | collective-permute-done | bytes 262176 | tf_op jit(solution)/shard_map/ppermute | solution.py:12
  105.2 9.2 %collective-permute-done.20 = f32[256,384]{0,1:T(8,128)S(1)} collective-permute-done((f32[256,384]{0,1:T(8,128)S(1)}, f32[256,384]{0,1:T(8,128)S(1)}, u32[]{:S(2)}, u32[]{:S(2)}) %collective-permute-start.20) | collective-permute-done | bytes 393248 | tf_op jit(solution)/shard_map/ppermute | solution.py:12
  150.2 5.2 %collective-permute-done.30 = bf16[8,128,128]{2,1,0:T(8,128)(2,1)S(1)} collective-permute-done((bf16[8,128,128]{2,1,0:T(8,128)(2,1)S(1)}, bf16[8,128,128]{2,1,0:T(8,128)(2,1)S(1)}, u32[]{:S(2)}, u32[]{:S(2)}) %collective-permute-start.30) | collective-permute-done | bytes 262176 | tf_op jit(solution)/shard_map/ppermute | solution.py:12
  163.0 4.3 %collective-permute-done.38 = bf16[4,128,256]{2,1,0:T(8,128)(2,1)S(1)} collective-permute-done((bf16[4,128,256]{2,1,0:T(8,128)(2,1)S(1)}, bf16[4,128,256]{2,1,0:T(8,128)(2,1)S(1)}, u32[]{:S(2)}, u32[]{:S(2)}) %collective-permute-start.38) | collective-permute-done | bytes 262176 | tf_op jit(solution)/shard_map/ppermute | solution.py:12
  173.1 5.6 %collective-permute-done.42 = bf16[4,128,256]{2,1,0:T(8,128)(2,1)S(1)} collective-permute-done((bf16[4,128,256]{2,1,0:T(8,128)(2,1)S(1)}, bf16[4,128,256]{2,1,0:T(8,128)(2,1)S(1)}, u32[]{:S(2)}, u32[]{:S(2)}) %collective-permute-start.42) | collective-permute-done | bytes 262176 | tf_op jit(solution)/shard_map/ppermute | solution.py:12
  190.7 6.4 %collective-permute-done.47 = f32[128,384]{1,0:T(8,128)S(1)} collective-permute-done((f32[128,384]{1,0:T(8,128)S(1)}, f32[128,384]{1,0:T(8,128)S(1)}, u32[]{:S(2)}, u32[]{:S(2)}) %collective-permute-start.47) | collective-permute-done | bytes 196640 | tf_op jit(solution)/shard_map/ppermute | solution.py:12
  220.8 4.9 %collective-permute-done.53 = bf16[64,128]{1,0:T(8,128)(2,1)S(1)} collective-permute-done((bf16[64,128]{1,0:T(8,128)(2,1)S(1)}, bf16[64,128]{1,0:T(8,128)(2,1)S(1)}, u32[]{:S(2)}, u32[]{:S(2)}) %collective-permute-start.53) | collective-permute-done | bytes 16416 | tf_op jit(solution)/shard_map/ppermute | solution.py:12
  240.5 3.9 collective-permute-done.67
  249.3 3.6 collective-permute-start.79
  258.6 4.1 %collective-permute-done.58 = bf16[4,64,128]{2,1,0:T(8,128)(2,1)S(1)} collective-permute-done((bf16[4,64,128]{2,1,0:T(8,128)(2,1)S(1)}, bf16[4,64,128]{2,1,0:T(8,128)(2,1)S(1)}, u32[]{:S(2)}, u32[]{:S(2)}) %collective-permute-start.58) | collective-permute-done | bytes 65568 | tf_op jit(solution)/shard_map/ppermute | solution.py:12
  270.4 4.2 %collective-permute-done.84 = bf16[2,4,64,128]{3,2,1,0:T(8,128)(2,1)S(1)} collective-permute-done((bf16[2,4,64,128]{3,2,1,0:T(8,128)(2,1)S(1)}, bf16[2,4,64,128]{3,2,1,0:T(8,128)(2,1)S(1)}, u32[]{:S(2)}, u32[]{:S(2)}) %collective-permute-start.84) | collective-permute-done | bytes 131104 | tf_op jit(solution)/shard_map/ppermute | solution.py:12
  289.1 4.4 %collective-permute-done.89 = f32[64,384]{1,0:T(8,128)S(1)} collective-permute-done((f32[64,384]{1,0:T(8,128)S(1)}, f32[64,384]{1,0:T(8,128)S(1)}, u32[]{:S(2)}, u32[]{:S(2)}) %collective-permute-start.89) | collective-permute-done | bytes 98336 | tf_op jit(solution)/shard_map/ppermute | solution.py:12
  320.2 4.8 %collective-permute-done.95 = bf16[32,128]{1,0:T(8,128)(2,1)S(1)} collective-permute-done((bf16[32,128]{1,0:T(8,128)(2,1)S(1)}, bf16[32,128]{1,0:T(8,128)(2,1)S(1)}, u32[]{:S(2)}, u32[]{:S(2)}) %collective-permute-start.95) | collective-permute-done | bytes 8224 | tf_op jit(solution)/shard_map/ppermute | solution.py:12
  347.2 3.7 collective-permute-done.115
  365.8 4.9 %collective-permute-done.134 = bf16[4,4,32,128]{3,2,1,0:T(8,128)(2,1)S(1)} collective-permute-done((bf16[4,4,32,128]{3,2,1,0:T(8,128)(2,1)S(1)}, bf16[4,4,32,128]{3,2,1,0:T(8,128)(2,1)S(1)}, u32[]{:S(2)}, u32[]{:S(2)}) %collective-permute-start.134) | collective-permute-done | bytes 131104 | tf_op jit(solution)/shard_map/ppermute | solution.py:12
  394.1 5.6 %collective-permute-start.141 = (f32[2,1,16,384]{3,2,1,0:T(8,128)S(1)}, f32[2,1,16,384]{3,2,1,0:T(8,128)S(1)}, u32[]{:S(2)}, u32[]{:S(2)}) collective-permute-start(f32[2,1,16,384]{3,2,1,0:T(8,128)S(1)} %get-tuple-element.48), channel_id=1, source_target_pairs={{8,0},{16,8},{24,16},{32,24},{40,32},{48,40},{56,48},{64,56},{72,6... | collective-permute-start | bytes 147464 | tf_op jit(solution)/shard_map/ppermute | solution.py:110
  403.5 4.3 %collective-permute-start.143 = (f32[2,4,1,384]{3,2,1,0:T(1,128)S(1)}, f32[2,4,1,384]{3,2,1,0:T(1,128)S(1)}, u32[]{:S(2)}, u32[]{:S(2)}) collective-permute-start(f32[2,4,1,384]{3,2,1,0:T(1,128)S(1)} %get-tuple-element.42), channel_id=1, source_target_pairs={{1,0},{2,1},{3,2},{4,3},{5,4},{6,5},{7,6},{9,8},{10,9},{11,10},{12... | collective-permute-start | bytes 36872 | tf_op jit(solution)/shard_map/ppermute | solution.py:110
  (543 shorter events, 284.9 us)
Async XLA Ops:
  2.1 37.3 %collective-permute-start = (bf16[256,128]{1,0:T(8,128)(2,1)}, bf16[256,128]{1,0:T(8,128)(2,1)}, u32[]{:S(2)}, u32[]{:S(2)}) collective-permute-start(bf16[256,128]{1,0:T(8,128)(2,1)} %slice.216), channel_id=1, source_target_pairs={{0,7},{1,0},{2,1},{3,2},{4,3},{5,4},{6,5},{7,6},{8,15},{9,8},{10,9... | collective-permute-start | bytes 196616 | tf_op jit(solution)/shard_map/ppermute | solution.py:12
  2.2 41.7 %collective-permute-start.3 = (bf16[256,128]{1,0:T(8,128)(2,1)}, bf16[256,128]{1,0:T(8,128)(2,1)S(1)}, u32[]{:S(2)}, u32[]{:S(2)}) collective-permute-start(bf16[256,128]{1,0:T(8,128)(2,1)} %slice.216), channel_id=1, source_target_pairs={{0,1},{1,2},{2,3},{3,4},{4,5},{5,6},{6,7},{7,0},{8,9},{9,10},{10,1... | collective-permute-start | bytes 196616 | tf_op jit(solution)/shard_map/ppermute | solution.py:12
  5.7 39.1 %collective-permute-start.9 = (bf16[256,256]{1,0:T(8,128)(2,1)}, bf16[256,256]{1,0:T(8,128)(2,1)S(1)}, u32[]{:S(2)}, u32[]{:S(2)}) collective-permute-start(bf16[256,256]{1,0:T(8,128)(2,1)} %get-tuple-element.46), channel_id=1, source_target_pairs={{0,16},{16,0},{32,48},{48,32},{1,17},{17,1},{33,49},{49,33},{2,18}... | collective-permute-start | bytes 393224 | tf_op jit(solution)/shard_map/ppermute | solution.py:12
  18.4 76.3 %collective-permute-start.18 = (bf16[256,4096]{0,1:T(8,128)(2,1)}, bf16[256,4096]{0,1:T(8,128)(2,1)}, u32[]{:S(2)}, u32[]{:S(2)}) collective-permute-start(bf16[256,4096]{0,1:T(8,128)(2,1)} %bitcast.37), channel_id=1, source_target_pairs={{0,8},{8,0},{1,9},{9,1},{2,10},{10,2},{3,11},{11,3},{4,12},{12,4},... | collective-permute-start | bytes 6291464 | tf_op jit(solution)/shard_map/ppermute | solution.py:12
  23.5 147.8 %collective-permute-start.45 = (bf16[128,4096]{0,1:T(8,128)(2,1)}, bf16[128,4096]{0,1:T(8,128)(2,1)}, u32[]{:S(2)}, u32[]{:S(2)}) collective-permute-start(bf16[128,4096]{0,1:T(8,128)(2,1)} %bitcast.66), channel_id=1, source_target_pairs={{0,8},{8,0},{1,9},{9,1},{2,10},{10,2},{3,11},{11,3},{4,12},{12,4},... | collective-permute-start | bytes 3145736 | tf_op jit(solution)/shard_map/ppermute | solution.py:12
  44.8 16.0 %collective-permute-start.10 = (bf16[2,256,256]{2,1,0:T(8,128)(2,1)S(1)}, bf16[2,256,256]{2,1,0:T(8,128)(2,1)S(1)}, u32[]{:S(2)}, u32[]{:S(2)}) collective-permute-start(bf16[2,256,256]{2,1,0:T(8,128)(2,1)S(1)} %pad_maximum_fusion.3), channel_id=1, source_target_pairs={{0,7},{1,0},{2,1},{3,2},{4,3},{5,4},{6,5},{7,6},{8,15},{9,8},{10,9... | collective-permute-start | bytes 786440 | tf_op jit(solution)/shard_map/ppermute | solution.py:12
  60.3 17.3 %collective-permute-start.8 = (bf16[8,256,128]{2,1,0:T(8,128)(2,1)S(1)}, bf16[8,256,128]{2,1,0:T(8,128)(2,1)S(1)}, u32[]{:S(2)}, u32[]{:S(2)}) collective-permute-start(bf16[8,256,128]{2,1,0:T(8,128)(2,1)S(1)} %constant_dynamic-update-slice_fusion), channel_id=1, source_target_pairs={{0,16},{16,0},{32,48},{48,32},{1,17},{17,1},{33,49},{49,33},{2,18}... | collective-permute-start | bytes 1572872 | tf_op jit(solution)/shard_map/ppermute | solution.py:12
  68.2 18.7 %collective-permute-start.12 = (bf16[2,256,256]{2,1,0:T(8,128)(2,1)S(1)}, bf16[2,256,256]{2,1,0:T(8,128)(2,1)S(1)}, u32[]{:S(2)}, u32[]{:S(2)}) collective-permute-start(bf16[2,256,256]{2,1,0:T(8,128)(2,1)S(1)} %collective-permute-done.11), channel_id=1, source_target_pairs={{0,7},{1,0},{2,1},{3,2},{4,3},{5,4},{6,5},{7,6},{8,15},{9,8},{10,9... | collective-permute-start | bytes 786440 | tf_op jit(solution)/shard_map/ppermute | solution.py:12
  127.6 153.8 %collective-permute-start.87 = (bf16[64,4096]{1,0:T(8,128)(2,1)S(1)}, bf16[64,4096]{1,0:T(8,128)(2,1)S(1)}, u32[]{:S(2)}, u32[]{:S(2)}) collective-permute-start(bf16[64,4096]{1,0:T(8,128)(2,1)S(1)} %bitcast.432), channel_id=1, source_target_pairs={{0,8},{8,0},{1,9},{9,1},{2,10},{10,2},{3,11},{11,3},{4,12},{12,4},... | collective-permute-start | bytes 1572872 | tf_op jit(solution)/shard_map/ppermute | solution.py:12
  209.1 18.2 %collective-permute-start.62 = (bf16[2,64,128]{2,1,0:T(8,128)(2,1)S(1)}, bf16[2,64,128]{2,1,0:T(8,128)(2,1)S(1)}, u32[]{:S(2)}, u32[]{:S(2)}) collective-permute-start(bf16[2,64,128]{2,1,0:T(8,128)(2,1)S(1)} %pad_maximum_fusion.13), channel_id=1, source_target_pairs={{0,7},{1,0},{2,1},{3,2},{4,3},{5,4},{6,5},{7,6},{8,15},{9,8},{10,9... | collective-permute-start | bytes 98312 | tf_op jit(solution)/shard_map/ppermute | solution.py:12
  212.7 17.9 %collective-permute-start.65 = (bf16[2,64,128]{2,1,0:T(8,128)(2,1)S(1)}, bf16[2,64,128]{2,1,0:T(8,128)(2,1)S(1)}, u32[]{:S(2)}, u32[]{:S(2)}) collective-permute-start(bf16[2,64,128]{2,1,0:T(8,128)(2,1)S(1)} %pad_maximum_fusion.13), channel_id=1, source_target_pairs={{0,1},{1,2},{2,3},{3,4},{4,5},{5,6},{6,7},{7,0},{8,9},{9,10},{10,1... | collective-permute-start | bytes 98312 | tf_op jit(solution)/shard_map/ppermute | solution.py:12
  233.9 19.0 %collective-permute-start.57 = (bf16[8,64,128]{2,1,0:T(8,128)(2,1)S(1)}, bf16[8,64,128]{2,1,0:T(8,128)(2,1)S(1)}, u32[]{:S(2)}, u32[]{:S(2)}) collective-permute-start(bf16[8,64,128]{2,1,0:T(8,128)(2,1)S(1)} %constant_dynamic-update-slice_fusion.18), channel_id=1, source_target_pairs={{0,16},{16,32},{32,48},{48,0},{1,17},{17,33},{33,49},{49,1},{2,18}... | collective-permute-start | bytes 393224 | tf_op jit(solution)/shard_map/ppermute | solution.py:12
  235.5 17.6 %collective-permute-start.56 = (bf16[8,64,128]{2,1,0:T(8,128)(2,1)S(1)}, bf16[8,64,128]{2,1,0:T(8,128)(2,1)S(1)}, u32[]{:S(2)}, u32[]{:S(2)}) collective-permute-start(bf16[8,64,128]{2,1,0:T(8,128)(2,1)S(1)} %constant_dynamic-update-slice_fusion.18), channel_id=1, source_target_pairs={{0,48},{16,0},{32,16},{48,32},{1,49},{17,1},{33,17},{49,33},{2,50}... | collective-permute-start | bytes 393224 | tf_op jit(solution)/shard_map/ppermute | solution.py:12
  252.9 16.8 %collective-permute-start.71 = (bf16[8,2,64,128]{3,2,1,0:T(8,128)(2,1)S(1)}, bf16[8,2,64,128]{3,2,1,0:T(8,128)(2,1)S(1)}, u32[]{:S(2)}, u32[]{:S(2)}) collective-permute-start(bf16[8,2,64,128]{3,2,1,0:T(8,128)(2,1)S(1)} %constant_dynamic-update-slice_fusion.26), channel_id=1, source_target_pairs={{0,16},{16,32},{32,48},{48,0},{1,17},{17,33},{33,49},{49,1},{2,18}... | collective-permute-start | bytes 786440 | tf_op jit(solution)/shard_map/ppermute | solution.py:12
  312.5 24.1 %collective-permute-start.110 = (bf16[4,32,128]{2,1,0:T(8,128)(2,1)S(1)}, bf16[4,32,128]{2,1,0:T(8,128)(2,1)S(1)}, u32[]{:S(2)}, u32[]{:S(2)}) collective-permute-start(bf16[4,32,128]{2,1,0:T(8,128)(2,1)S(1)} %pad_maximum_fusion.14), channel_id=1, source_target_pairs={{0,7},{1,0},{2,1},{3,2},{4,3},{5,4},{6,5},{7,6},{8,15},{9,8},{10,9... | collective-permute-start | bytes 98312 | tf_op jit(solution)/shard_map/ppermute | solution.py:12
  315.8 23.0 %collective-permute-start.113 = (bf16[4,32,128]{2,1,0:T(8,128)(2,1)S(1)}, bf16[4,32,128]{2,1,0:T(8,128)(2,1)S(1)}, u32[]{:S(2)}, u32[]{:S(2)}) collective-permute-start(bf16[4,32,128]{2,1,0:T(8,128)(2,1)S(1)} %pad_maximum_fusion.14), channel_id=1, source_target_pairs={{0,1},{1,2},{2,3},{3,4},{4,5},{5,6},{6,7},{7,0},{8,9},{9,10},{10,1... | collective-permute-start | bytes 98312 | tf_op jit(solution)/shard_map/ppermute | solution.py:12
  315.8 16.3 %collective-permute-start.127 = (bf16[4,32,128]{2,1,0:T(8,128)(2,1)S(1)}, bf16[4,32,128]{2,1,0:T(8,128)(2,1)S(1)}, u32[]{:S(2)}, u32[]{:S(2)}) collective-permute-start(bf16[4,32,128]{2,1,0:T(8,128)(2,1)S(1)} %get-tuple-element.59), channel_id=1, source_target_pairs={{0,64},{64,128},{128,192},{192,0},{1,65},{65,129},{129,193},{193,1... | collective-permute-start | bytes 98312 | tf_op jit(solution)/shard_map/ppermute | solution.py:12
  332.1 15.0 %collective-permute-start.99 = (bf16[8,32,128]{2,1,0:T(8,128)(2,1)S(1)}, bf16[8,32,128]{2,1,0:T(8,128)(2,1)S(1)}, u32[]{:S(2)}, u32[]{:S(2)}) collective-permute-start(bf16[8,32,128]{2,1,0:T(8,128)(2,1)S(1)} %constant_dynamic-update-slice_fusion.42), channel_id=1, source_target_pairs={{0,16},{16,32},{32,48},{48,0},{1,17},{17,33},{33,49},{49,1},{2,18}... | collective-permute-start | bytes 196616 | tf_op jit(solution)/shard_map/ppermute | solution.py:12
  332.2 15.0 %collective-permute-start.98 = (bf16[8,32,128]{2,1,0:T(8,128)(2,1)S(1)}, bf16[8,32,128]{2,1,0:T(8,128)(2,1)S(1)}, u32[]{:S(2)}, u32[]{:S(2)}) collective-permute-start(bf16[8,32,128]{2,1,0:T(8,128)(2,1)S(1)} %constant_dynamic-update-slice_fusion.42), channel_id=1, source_target_pairs={{0,48},{16,0},{32,16},{48,32},{1,49},{17,1},{33,17},{49,33},{2,50}... | collective-permute-start | bytes 196616 | tf_op jit(solution)/shard_map/ppermute | solution.py:12
  342.2 16.8 %collective-permute-start.130 = (bf16[4,4,32,128]{3,2,1,0:T(8,128)(2,1)S(1)}, bf16[4,4,32,128]{3,2,1,0:T(8,128)(2,1)S(1)}, u32[]{:S(2)}, u32[]{:S(2)}) collective-permute-start(bf16[4,4,32,128]{3,2,1,0:T(8,128)(2,1)S(1)} %pad_maximum_fusion.8), channel_id=1, source_target_pairs={{0,7},{1,0},{2,1},{3,2},{4,3},{5,4},{6,5},{7,6},{8,15},{9,8},{10,9... | collective-permute-start | bytes 393224 | tf_op jit(solution)/shard_map/ppermute | solution.py:12
  347.0 17.2 %collective-permute-start.133 = (bf16[4,4,32,128]{3,2,1,0:T(8,128)(2,1)S(1)}, bf16[4,4,32,128]{3,2,1,0:T(8,128)(2,1)S(1)}, u32[]{:S(2)}, u32[]{:S(2)}) collective-permute-start(bf16[4,4,32,128]{3,2,1,0:T(8,128)(2,1)S(1)} %pad_maximum_fusion.8), channel_id=1, source_target_pairs={{0,1},{1,2},{2,3},{3,4},{4,5},{5,6},{6,7},{7,0},{8,9},{9,10},{10,1... | collective-permute-start | bytes 393224 | tf_op jit(solution)/shard_map/ppermute | solution.py:12
  355.3 18.2 %collective-permute-start.103 = (bf16[4,8,32,128]{3,2,1,0:T(8,128)(2,1)S(1)}, bf16[4,8,32,128]{3,2,1,0:T(8,128)(2,1)S(1)}, u32[]{:S(2)}, u32[]{:S(2)}) collective-permute-start(bf16[4,8,32,128]{3,2,1,0:T(8,128)(2,1)S(1)} %get-tuple-element.39), channel_id=1, source_target_pairs={{0,64},{64,128},{128,192},{192,0},{1,65},{65,129},{129,193},{193,1... | collective-permute-start | bytes 786440 | tf_op jit(solution)/shard_map/ppermute | solution.py:12
  356.7 16.8 %collective-permute-start.102 = (bf16[4,8,32,128]{3,2,1,0:T(8,128)(2,1)S(1)}, bf16[4,8,32,128]{3,2,1,0:T(8,128)(2,1)S(1)}, u32[]{:S(2)}, u32[]{:S(2)}) collective-permute-start(bf16[4,8,32,128]{3,2,1,0:T(8,128)(2,1)S(1)} %get-tuple-element.39), channel_id=1, source_target_pairs={{0,192},{64,0},{128,64},{192,128},{1,193},{65,1},{129,65},{193,129... | collective-permute-start | bytes 786440 | tf_op jit(solution)/shard_map/ppermute | solution.py:12
  373.5 16.2 %collective-permute-start.138 = (bf16[32,4096]{1,0:T(8,128)(2,1)S(1)}, bf16[32,4096]{1,0:T(8,128)(2,1)S(1)}, u32[]{:S(2)}, u32[]{:S(2)}) collective-permute-start(bf16[32,4096]{1,0:T(8,128)(2,1)S(1)} %bitcast.443), channel_id=1, source_target_pairs={{0,8},{8,0},{1,9},{9,1},{2,10},{10,2},{3,11},{11,3},{4,12},{12,4},... | collective-permute-start | bytes 786440 | tf_op jit(solution)/shard_map/ppermute | solution.py:12
  (131 other events, 1003.4 us)
